TPU v7x, 128 devices: a whole 4x4x4 slice. The times are simulated.
128 devices in a mesh: ctx: 4 (over x_hi, core), exp: 32 (over z, y, x_lo).
Axes of the slice: x: 4 (x_hi: 2, x_lo: 2; x = x_hi * 2 + x_lo), y: 4, z: 4, core: 2. Of those that a mesh axis runs over, the one named last changes fastest.
Arguments:
- queries: bfloat16 [4096, 8192], P('ctx', 'exp'), may hold values from -32 to 32
- keys: bfloat16 [4096, 8192], P('ctx', 'exp'), may hold values from -4 to 4
- values: bfloat16 [4096, 8192], P('ctx', 'exp'), may hold values from -6 to 6
- out_proj: bfloat16 [8192, 3584], P('exp'), may hold values from -0.5 to 0.5
- residual: bfloat16 [4096, 3584], P(('ctx', 'exp')), may hold values from -6 to 6
- norm_gain: float32 [3584], replicated, may hold values from 0.25 to 1.75
- routes: int32 [4096, 8], P(('ctx', 'exp')), may hold values from 0 to 31, all different within a row; in each aligned block of 32 rows (0 to 31, 32 to 63, ...) at most 10 rows name the same one
- combine: float32 [4096, 8], P(('ctx', 'exp')), may hold values from 0.1 to 0.5
- w_gate: bfloat16 [32, 3584, 1024], P('exp', None, 'ctx'), may hold values from -0.09375 to 0.09375
- w_up: bfloat16 [32, 3584, 1024], P('exp', None, 'ctx'), may hold values from -0.09375 to 0.09375
- w_down: bfloat16 [32, 1024, 3584], P('exp', 'ctx'), may hold values from -0.1875 to 0.1875
Outputs:
- layer_out: bfloat16 [4096, 3584], P(('ctx', 'exp'))
Inputs may be any that keep to these rules, and one draw needn't show every extreme that they name: `routes`: each row names 8 different experts. Within each aligned block of 32 rows no expert is named by more than 10 rows, and some block names some expert exactly 10 times.
All inputs are finite; a program needn't handle non-finite values.
Results may differ from a plain program's by a relative error of at most 0.023.
Values may be sent and summed in bfloat16 or wider, within the bound.
No kernel may reach another device: no remote copies, remote signals or barrier semaphores. Data moves between devices by JAX's collectives and lax.ppermute only.
A program may use at most 128 MiB of HBM per device.

v0:
```python
import math
import jax
import jax.numpy as jnp
from jax import lax
from jax.sharding import PartitionSpec as P

HD = 128
masked_score = -1e30
norm_eps = 1e-06


def from_behind(shard, axis, by):
    peers = lax.axis_size(axis)
    pairs = [(i, i + by) for i in range(peers) if 0 <= i + by < peers]
    return lax.ppermute(shard, axis, pairs)


def per_device(
    queries, keys, values, out_proj, residual, norm_gain, routes, combine, w_gate, w_up, w_down
):
    query_rows = queries.shape[0]
    head_count = queries.shape[1] // HD
    scaling = 1.0 / math.sqrt(HD)
    ctx_where = lax.axis_index("ctx")
    ctx_count = lax.axis_size("ctx")

    def attend(carried, query_heads, pair_block, visible):
        key_count = pair_block.shape[1]
        key_heads = pair_block[0].reshape(key_count, head_count, HD)
        value_heads = pair_block[1].reshape(key_count, head_count, HD)
        scores = (
            jnp.einsum("qhd,khd->hqk", query_heads, key_heads, preferred_element_type=jnp.float32)
            * scaling
        )
        scores = jnp.where(visible, scores, masked_score)
        peak_old, total_old, weighted_old = carried
        peak_new = jnp.maximum(peak_old, jnp.max(scores, axis=2))
        expo_block = jnp.exp(scores - peak_new[:, :, None])
        factor = jnp.exp(peak_old - peak_new)
        total_new = total_old * factor + jnp.sum(expo_block, axis=2)
        weighted_new = weighted_old * factor.T[:, :, None] + jnp.einsum(
            "hqk,khd->qhd",
            expo_block.astype(jnp.bfloat16),
            value_heads,
            preferred_element_type=jnp.float32,
        )
        return (peak_new, total_new, weighted_new)

    initial = (
        jnp.full((head_count, query_rows), masked_score, jnp.float32),
        jnp.zeros((head_count, query_rows), jnp.float32),
        jnp.zeros((query_rows, head_count, HD), jnp.float32),
    )
    query_heads = queries.reshape(query_rows, head_count, HD)
    row_ids = jnp.arange(query_rows)
    diag_mask = row_ids[:, None] >= row_ids[None, :]
    pair_block = jnp.stack([keys, values])
    carried = attend(initial, query_heads, pair_block, diag_mask)
    for step_index in range(1, ctx_count):
        pair_block = from_behind(pair_block, "ctx", 1)
        carried = attend(carried, query_heads, pair_block, ctx_where >= step_index)
    attended = (
        (carried[2] / carried[1].T[:, :, None])
        .astype(jnp.bfloat16)
        .reshape(query_rows, head_count * HD)
    )
    tok_count = residual.shape[0]
    term = jnp.dot(attended, out_proj, preferred_element_type=jnp.float32)
    mixed = lax.psum_scatter(
        lax.optimization_barrier(term.astype(jnp.bfloat16))
        .astype(jnp.float32)
        .astype(jnp.bfloat16),
        "exp",
        scatter_dimension=0,
        tiled=True,
    ).astype(jnp.float32)
    stream = residual.astype(jnp.float32) + mixed
    normed = (
        stream * lax.rsqrt(jnp.mean(stream * stream, axis=1, keepdims=True) + norm_eps) * norm_gain
    ).astype(jnp.bfloat16)
    width = normed.shape[1]
    per_token = routes.shape[1]
    experts = lax.axis_size("exp")
    capacity = min(tok_count, max(2, tok_count * per_token * 5 // (4 * experts)))
    pair_count = tok_count * per_token
    flat_routes = routes.reshape(pair_count)
    expert_hot = (flat_routes[:, None] == jnp.arange(experts)[None, :]).astype(jnp.int32)
    earlier = jnp.cumsum(expert_hot, axis=0) - expert_hot
    slot_index = jnp.sum(earlier * expert_hot, axis=1)
    position = flat_routes * capacity + slot_index
    position_hot = (position[:, None] == jnp.arange(experts * capacity)[None, :]).astype(
        jnp.float32
    )
    token_hot = (
        (jnp.arange(pair_count) // per_token)[:, None] == jnp.arange(tok_count)[None, :]
    ).astype(jnp.float32)
    pick_rows = jnp.einsum("pr,pt->rt", position_hot, token_hot).astype(jnp.bfloat16)
    outgoing = (
        jnp.dot(pick_rows, normed, preferred_element_type=jnp.float32)
        .astype(jnp.bfloat16)
        .reshape(experts, capacity, width)
    )
    received = lax.all_to_all(outgoing, "exp", split_axis=0, concat_axis=0, tiled=True)
    gate_local = w_gate[0]
    up_local = w_up[0]
    down_local = w_down[0]
    piece = lax.all_gather(received, "ctx", axis=0, tiled=True)
    gate = jnp.einsum("smd,df->smf", piece, gate_local, preferred_element_type=jnp.float32)
    upper = jnp.einsum("smd,df->smf", piece, up_local, preferred_element_type=jnp.float32)
    act_all = (jax.nn.silu(gate) * upper).astype(jnp.bfloat16)
    expert_out = lax.psum_scatter(
        jnp.einsum("smf,fd->smd", act_all, down_local, preferred_element_type=jnp.float32).astype(
            jnp.bfloat16
        ),
        "ctx",
        scatter_dimension=0,
        tiled=True,
    )
    returned = lax.all_to_all(expert_out, "exp", split_axis=0, concat_axis=0, tiled=True)
    weigh_rows = jnp.einsum(
        "pr,pt->tr", position_hot, token_hot * combine.reshape(pair_count)[:, None]
    )
    moe_sum = jnp.dot(
        weigh_rows,
        returned.reshape(experts * capacity, width).astype(jnp.float32),
        precision=lax.Precision.HIGHEST,
    )
    return (stream + moe_sum).astype(jnp.bfloat16)


def solution(mesh):
    in_specs = (
        P("ctx", "exp"),
        P("ctx", "exp"),
        P("ctx", "exp"),
        P("exp", None),
        P(("ctx", "exp"), None),
        P(),
        P(("ctx", "exp"), None),
        P(("ctx", "exp"), None),
        P("exp", None, "ctx"),
        P("exp", None, "ctx"),
        P("exp", "ctx", None),
    )
    out_specs = P(("ctx", "exp"), None)
    return jax.shard_map(
        per_device, mesh=mesh, in_specs=in_specs, out_specs=out_specs, check_vma=False
    )
```

profile of v0, /device:TPU:0, one launch (start us, length us, event | category | flops | bytes accessed | tf_op | source)
XLA Modules:
  0.0 577.8 jit_solution(9103200832604221513)
XLA Ops:
  9.3 2.5 collective-permute-start
  13.1 16.1 %collective-permute-start.1 = (bf16[2,1024,256]{1,2,0:T(8,128)(2,1)}, bf16[2,1024,256]{1,2,0:T(8,128)(2,1)}, u32[]{:S(2)}, u32[]{:S(2)}) collective-permute-start(bf16[2,1024,256]{1,2,0:T(8,128)(2,1)} %collective-permute-done), channel_id=1, source_target_pairs={{0,32},{32,64},{64,96},{1,33},{33,65},{65,97},{2,34},{34,66},{66,9... | collective-permute-start | bytes 3145736 | tf_op jit(solution)/shard_map/ppermute | solution.py:15
  29.5 6.3 %fusion.3 = (f32[2,1024]{1,0:T(2,128)S(1)}, f32[2,1024,1024]{1,2,0:T(8,128)}) fusion(pred[1024,1024]{0,1:T(8,128)(4,1)S(1)} %iota_compare_fusion, bf16[1024,256]{1,0:T(8,128)(2,1)} %param.12, bf16[1024,256]{1,0:T(8,128)(2,1)} %param.11), kind=kOutput, calls=%fused_computation.16 | convolution fusion | flops 543160320 | bytes 10493952 | tf_op jit(solution)/shard_map/qhd,khd->hqk/dot_general | solution.py:32
  37.1 9.3 %collective-permute-start.2 = (bf16[2,1024,256]{1,2,0:T(8,128)(2,1)}, bf16[2,1024,256]{1,2,0:T(8,128)(2,1)S(1)}, u32[]{:S(2)}, u32[]{:S(2)}) collective-permute-start(bf16[2,1024,256]{1,2,0:T(8,128)(2,1)} %collective-permute-done.1), channel_id=1, source_target_pairs={{0,32},{32,64},{64,96},{1,33},{33,65},{65,97},{2,34},{34,66},{66,9... | collective-permute-start | bytes 3145736 | tf_op jit(solution)/shard_map/ppermute | solution.py:15
  54.3 4.5 fusion.4
  58.8 4.0 fusion.6
  62.9 4.9 fusion.66
  67.7 2.6 fusion.57
  70.4 2.6 fusion.60
  75.5 5.1 convolution_convert_fusion.1
  81.8 201.2 %reduce-scatter.3.cloned.1.call-done = bf16[32,3584]{1,0:T(8,128)(2,1)} async-done(((bf16[1024,3584]{1,0:T(8,128)(2,1)}), bf16[32,3584]{1,0:T(8,128)(2,1)}) %reduce-scatter.3.cloned.1.call-update) | async-done | bytes 229392 | tf_op jit(solution)/shard_map/reduce_scatter | solution.py:69
  284.2 3.4 convolution_convert_fusion.2
  287.6 4.4 reshape.96
  292.0 33.5 %all_to_all.10 = bf16[32,10,3584]{2,1,0:T(8,128)(2,1)S(1)} all-to-all(bf16[32,10,3584]{2,1,0:T(8,128)(2,1)} %reshape.96), channel_id=1, replica_groups=mesh['ctx'=4,'exp'=32] {'exp'}, dimensions={0} | all-to-all | bytes 4587520 | tf_op jit(solution)/shard_map/all_to_all | solution.py:103
  325.5 2.7 copy.66
  328.2 64.2 %all-gather.2.cloned.1.call-done = bf16[128,10,3584]{2,0,1:T(8,128)(2,1)} async-done(((bf16[32,10,3584]{2,0,1:T(8,128)(2,1)}), bf16[128,10,3584]{2,0,1:T(8,128)(2,1)}) %all-gather.2.cloned.1.call-update) | async-done | bytes 9175056 | tf_op jit(solution)/shard_map/all_gather | solution.py:107
  392.4 7.7 %fusion.28 = f32[128,10,256]{2,0,1:T(8,128)} fusion(bf16[128,10,3584]{2,0,1:T(8,128)(2,1)} %all-gather.2.cloned.1.call-done, bf16[1,3584,256]{2,1,0:T(8,128)(2,1)} %param.19), kind=kOutput, calls=%fused_computation.40 | convolution fusion | flops 2348810240 | bytes 12320768 | tf_op jit(solution)/shard_map/smd,df->smf/dot_general | solution.py:108
  400.2 18.5 %convolution_convert_fusion = bf16[128,10,3584]{2,0,1:T(8,128)(2,1)} fusion(bf16[1,256,3584]{2,1,0:T(8,128)(2,1)S(1)} %copy-done, bf16[128,10,3584]{2,0,1:T(8,128)(2,1)} %all-gather.2.cloned.1.call-done, bf16[1,3584,256]{2,1,0:T(8,128)(2,1)} %param.20, f32[128,10,256]{2,0,1:T(8,128)} %fusion.28), kind=kOutput, calls=%fused_computation.14 | convolution fusion | flops 4704174080 | bytes 23330816 | tf_op jit(solution)/shard_map/smf,fd->smd/dot_general | solution.py:112
  418.7 82.6 %reduce-scatter.5.cloned.1.call-done = bf16[32,10,3584]{2,0,1:T(8,128)(2,1)} async-done(((bf16[128,10,3584]{2,0,1:T(8,128)(2,1)}), bf16[32,10,3584]{2,0,1:T(8,128)(2,1)}) %reduce-scatter.5.cloned.1.call-update) | async-done | bytes 2293776 | tf_op jit(solution)/shard_map/reduce_scatter | solution.py:111
  501.3 4.9 copy.67
  506.1 7.4 %all-to-all-start.1 = ((bf16[32,10,3584]{2,1,0:T(8,128)(2,1)}), bf16[32,10,3584]{2,1,0:T(8,128)(2,1)}, u32[]{:S(2)}, u32[]{:S(2)}) async-start(bf16[32,10,3584]{2,1,0:T(8,128)(2,1)} %copy.67), calls=%async_computation.3 | async-start | bytes 7340032 | tf_op jit(solution)/shard_map/all_to_all | solution.py:119
  514.0 49.2 %all-to-all-done.1 = bf16[32,10,3584]{2,1,0:T(8,128)(2,1)} async-done(((bf16[32,10,3584]{2,1,0:T(8,128)(2,1)}), bf16[32,10,3584]{2,1,0:T(8,128)(2,1)}, u32[]{:S(2)}, u32[]{:S(2)}) %all-to-all-start.1) | async-done | bytes 2293792 | tf_op jit(solution)/shard_map/all_to_all | solution.py:119
  563.2 4.5 reshape.97
  567.7 3.6 fusion.12
  (54 shorter events, 19.0 us)
Async XLA Ops:
  6.5 393.6 %copy-start = (bf16[1,256,3584]{2,1,0:T(8,128)(2,1)S(1)}, bf16[1,256,3584]{2,1,0:T(8,128)(2,1)}, u32[]{:S(2)}) copy-start(bf16[1,256,3584]{2,1,0:T(8,128)(2,1)} %param.21) | copy-start | bytes 5505028
  6.5 276.5 %reduce-scatter.3.cloned.1.call-start = ((), (), s32[]{:S(2)}) async-start(), calls=%async_computation.4 | async-start | bytes 7569408 | tf_op jit(solution)/shard_map/reduce_scatter | solution.py:69
  9.2 37.1 %copy-start.1 = (bf16[1024,256]{1,0:T(8,128)(2,1)S(1)}, bf16[1024,256]{1,0:T(8,128)(2,1)}, u32[]{:S(2)}) copy-start(bf16[1024,256]{1,0:T(8,128)(2,1)} %param.11) | copy-start | bytes 1572868
  9.3 3.8 collective-permute-start
  13.1 23.9 %collective-permute-start.1 = (bf16[2,1024,256]{1,2,0:T(8,128)(2,1)}, bf16[2,1024,256]{1,2,0:T(8,128)(2,1)}, u32[]{:S(2)}, u32[]{:S(2)}) collective-permute-start(bf16[2,1024,256]{1,2,0:T(8,128)(2,1)} %collective-permute-done), channel_id=1, source_target_pairs={{0,32},{32,64},{64,96},{1,33},{33,65},{65,97},{2,34},{34,66},{66,9... | collective-permute-start | bytes 3145736 | tf_op jit(solution)/shard_map/ppermute | solution.py:15
  37.1 13.4 %collective-permute-start.2 = (bf16[2,1024,256]{1,2,0:T(8,128)(2,1)}, bf16[2,1024,256]{1,2,0:T(8,128)(2,1)S(1)}, u32[]{:S(2)}, u32[]{:S(2)}) collective-permute-start(bf16[2,1024,256]{1,2,0:T(8,128)(2,1)} %collective-permute-done.1), channel_id=1, source_target_pairs={{0,32},{32,64},{64,96},{1,33},{33,65},{65,97},{2,34},{34,66},{66,9... | collective-permute-start | bytes 3145736 | tf_op jit(solution)/shard_map/ppermute | solution.py:15
  73.0 2.4 copy-start.4
  75.4 5.2 copy-start.6
  75.4 207.6 %copy-start.2 = (bf16[32,3584]{1,0:T(8,128)(2,1)S(1)}, bf16[32,3584]{1,0:T(8,128)(2,1)}, u32[]{:S(2)}) copy-start(bf16[32,3584]{1,0:T(8,128)(2,1)} %param.15) | copy-start | bytes 688132
  75.5 208.8 %copy-start.5 = (f32[3584]{0:T(1024)S(1)}, f32[3584]{0:T(1024)}, u32[]{:S(2)}) copy-start(f32[3584]{0:T(1024)} %param.16) | copy-start | bytes 43012
  80.6 311.9 %all-gather.2.cloned.1.call-start = ((), (), s32[]{:S(2)}) async-start(), calls=%async_computation.5 | async-start | bytes 11468800 | tf_op jit(solution)/shard_map/all_gather | solution.py:107
  328.2 173.1 %reduce-scatter.5.cloned.1.call-start = ((), (), s32[]{:S(2)}) async-start(), calls=%async_computation.6 | async-start | bytes 11468800 | tf_op jit(solution)/shard_map/reduce_scatter | solution.py:111
  418.6 94.9 %copy-start.7 = (f32[32,8]{0,1:T(8,128)S(1)}, f32[32,8]{0,1:T(8,128)}, u32[]{:S(2)}) copy-start(f32[32,8]{0,1:T(8,128)} %param.18) | copy-start | bytes 3076
  418.7 149.1 %copy-start.3 = (bf16[32,3584]{1,0:T(8,128)(2,1)S(1)}, bf16[32,3584]{1,0:T(8,128)(2,1)}, u32[]{:S(2)}) copy-start(bf16[32,3584]{1,0:T(8,128)(2,1)} %reduce-scatter.3.cloned.1.call-done) | copy-start | bytes 688132
  506.1 57.1 %all-to-all-start.1 = ((bf16[32,10,3584]{2,1,0:T(8,128)(2,1)}), bf16[32,10,3584]{2,1,0:T(8,128)(2,1)}, u32[]{:S(2)}, u32[]{:S(2)}) async-start(bf16[32,10,3584]{2,1,0:T(8,128)(2,1)} %copy.67), calls=%async_computation.3 | async-start | bytes 7340032 | tf_op jit(solution)/shard_map/all_to_all | solution.py:119
Sparse Core Ops, SparseCore 0:
  80.7 202.3 reduce-scatter.2
  328.3 64.0 all-gather.1
  418.8 82.4 reduce-scatter.4
where the time goes:
time: 579 us; the launch traced here: 578 us
  waiting for transfers between devices  399 us (69%)
  matrix products  61.7 us (11%)
  starting transfers between devices  35.3 us (6%)
  blocking collectives  33.5 us (6%)
  local copies, waits for them, and re-layouts  22.3 us (4%)
  between operations  13.4 us (2%)
  other arithmetic  13.1 us (2%)
    reduce_scatter x1, waiting for transfers between devices, per_device(): lax.psum_scatter(lax.optimization_barrier(term.astype(jnp.bfloat16)).asty...  201 us
    reduce_scatter x1, waiting for transfers between devices, per_device(): lax.psum_scatter(jnp.einsum('smf,fd->smd', act_all, down_local, preferred...  82.6 us
    all_gather x1, waiting for transfers between devices, per_device(): piece = lax.all_gather(received, 'ctx', axis=0, tiled=True)  64.2 us
    all_to_all x1, waiting for transfers between devices, per_device(): lax.all_to_all(expert_out, 'exp', split_axis=0, concat_axis=0, tiled=True)  49.2 us
    all_to_all x1, blocking collectives, per_device(): lax.all_to_all(outgoing, 'exp', split_axis=0, concat_axis=0, tiled=True)  33.5 us
    ppermute x3, starting transfers between devices, from_behind(): return lax.ppermute(shard, axis, pairs)  27.8 us
    dot_general x1, matrix products, per_device(): jnp.einsum('smf,fd->smd', act_all, down_local, preferred_element_type=jnp...  18.5 us
    dot_general x4, matrix products, attend(): jnp.einsum('hqk,khd->qhd', expo_block.astype(jnp.bfloat16), value_heads,...  12.5 us
  transfers between devices with their start and end apart: 7, of which 5 were waited for; matrix products, arithmetic and copies ran while one was open for 2% of the time, Pallas kernels for 0%

commit v1 on v0

--- a/solution.py
+++ b/solution.py
@@ -104,7 +104,9 @@
     gate_local = w_gate[0]
     up_local = w_up[0]
     down_local = w_down[0]
-    piece = lax.all_gather(received, "ctx", axis=0, tiled=True)
+    r2 = lax.axis_size("ctx")
+    n_now = lax.all_to_all(jnp.stack(r2 * [received]), axis_name="ctx", split_axis=0, concat_axis=0)
+    piece = jnp.concatenate(n_now, axis=0)
     gate = jnp.einsum("smd,df->smf", piece, gate_local, preferred_element_type=jnp.float32)
     upper = jnp.einsum("smd,df->smf", piece, up_local, preferred_element_type=jnp.float32)
     act_all = (jax.nn.silu(gate) * upper).astype(jnp.bfloat16)

time: 579 us -> 628 us (1.085)
  blocking collectives: 33.5 us -> 140 us
  waiting for transfers between devices: 399 us -> 330 us
  local copies, waits for them, and re-layouts: 22.3 us -> 33.2 us
    all_to_all x0 -> x1, blocking collectives: none -> 107 us  [per_device(): lax.all_to_all(jnp.stack(r2 * [received]), axis_name='ctx', split_axis=0,...]
    all_gather x1 -> x0, waiting for transfers between devices: 64.2 us -> none  [per_device(): piece = lax.all_gather(received, 'ctx', axis=0, tiled=True)]
    all_to_all x0 -> x1, local copies, waits for them, and re-layouts: none -> 8.15 us  [per_device(): lax.all_to_all(jnp.stack(r2 * [received]), axis_name='ctx', split_axis=0,...]
  transfers between devices with their start and end apart: 7 -> 6, of which waited for: 5 -> 4; matrix products, arithmetic and copies ran while one was open for 2% -> 2% of each run, Pallas kernels for 0% -> 0%
where the time goes in v1:
time: 628 us
  waiting for transfers between devices  330 us (53%)
  blocking collectives  140 us (22%)
  matrix products  61.7 us (10%)
  starting transfers between devices  35.3 us (6%)
  local copies, waits for them, and re-layouts  33.2 us (5%)
  between operations  13.7 us (2%)
  other arithmetic  13.1 us (2%)
    reduce_scatter x1, waiting for transfers between devices, per_device(): lax.psum_scatter(lax.optimization_barrier(term.astype(jnp.bfloat16)).asty...  201 us
    all_to_all x1, blocking collectives, per_device(): lax.all_to_all(jnp.stack(r2 * [received]), axis_name='ctx', split_axis=0,...  107 us
    reduce_scatter x1, waiting for transfers between devices, per_device(): lax.psum_scatter(jnp.einsum('smf,fd->smd', act_all, down_local, preferred...  78.5 us
    all_to_all x1, waiting for transfers between devices, per_device(): lax.all_to_all(expert_out, 'exp', split_axis=0, concat_axis=0, tiled=True)  49.3 us
    all_to_all x1, blocking collectives, per_device(): lax.all_to_all(outgoing, 'exp', split_axis=0, concat_axis=0, tiled=True)  33.5 us
    ppermute x3, starting transfers between devices, from_behind(): return lax.ppermute(shard, axis, pairs)  27.8 us
    dot_general x1, matrix products, per_device(): jnp.einsum('smf,fd->smd', act_all, down_local, preferred_element_type=jnp...  18.5 us
  transfers between devices with their start and end apart: 6, of which 4 were waited for; matrix products, arithmetic and copies ran while one was open for 2% of the time, Pallas kernels for 0%

profile of v1, /device:TPU:0, one launch (start us, length us, event | category | flops | bytes accessed | tf_op | source)
XLA Modules:
  0.0 627.5 jit_solution(12059499278909528783)
XLA Ops:
  13.1 16.1 %collective-permute-start.1 = (bf16[2,1024,256]{1,2,0:T(8,128)(2,1)}, bf16[2,1024,256]{1,2,0:T(8,128)(2,1)}, u32[]{:S(2)}, u32[]{:S(2)}) collective-permute-start(bf16[2,1024,256]{1,2,0:T(8,128)(2,1)} %collective-permute-done), channel_id=1, source_target_pairs={{0,32},{32,64},{64,96},{1,33},{33,65},{65,97},{2,34},{34,66},{66,9... | collective-permute-start | bytes 3145736 | tf_op jit(solution)/shard_map/ppermute | solution.py:15
  29.5 6.3 fusion.3
  37.1 9.3 %collective-permute-start.2 = (bf16[2,1024,256]{1,2,0:T(8,128)(2,1)}, bf16[2,1024,256]{1,2,0:T(8,128)(2,1)S(1)}, u32[]{:S(2)}, u32[]{:S(2)}) collective-permute-start(bf16[2,1024,256]{1,2,0:T(8,128)(2,1)} %collective-permute-done.1), channel_id=1, source_target_pairs={{0,32},{32,64},{64,96},{1,33},{33,65},{65,97},{2,34},{34,66},{66,9... | collective-permute-start | bytes 3145736 | tf_op jit(solution)/shard_map/ppermute | solution.py:15
  54.3 4.5 fusion.4
  58.8 4.0 fusion.6
  62.9 4.9 fusion.66
  70.4 2.6 fusion.60
  75.5 5.1 convolution_convert_fusion.1
  81.8 201.2 %reduce-scatter.3.cloned.1.call-done = bf16[32,3584]{1,0:T(8,128)(2,1)} async-done(((bf16[1024,3584]{1,0:T(8,128)(2,1)}), bf16[32,3584]{1,0:T(8,128)(2,1)}) %reduce-scatter.3.cloned.1.call-update) | async-done | bytes 229392 | tf_op jit(solution)/shard_map/reduce_scatter | solution.py:69
  284.2 3.4 convolution_convert_fusion.2
  287.6 4.4 reshape.101
  292.0 33.5 %all_to_all.15 = bf16[32,10,3584]{2,1,0:T(8,128)(2,1)S(1)} all-to-all(bf16[32,10,3584]{2,1,0:T(8,128)(2,1)} %reshape.101), channel_id=1, replica_groups=mesh['ctx'=4,'exp'=32] {'exp'}, dimensions={0} | all-to-all | bytes 4587520 | tf_op jit(solution)/shard_map/all_to_all | solution.py:103
  325.5 2.6 copy.66
  328.1 2.7 stack.19
  330.9 106.9 %all_to_all.16 = bf16[4,32,10,3584]{3,1,2,0:T(8,128)(2,1)} all-to-all(bf16[4,32,10,3584]{3,1,2,0:T(8,128)(2,1)S(1)} %stack.19), channel_id=1, replica_groups=mesh['ctx'=4,'exp'=32] {'ctx'}, dimensions={0} | all-to-all | bytes 18350080 | tf_op jit(solution)/shard_map/all_to_all | solution.py:108
  437.7 8.2 %copy.67 = bf16[4,32,10,3584]{3,1,0,2:T(8,128)(2,1)} copy(bf16[4,32,10,3584]{3,1,2,0:T(8,128)(2,1)} %all_to_all.16) | data formatting | bytes 18350080 | tf_op jit(solution)/shard_map/all_to_all | solution.py:108
  445.9 7.7 %fusion.28 = f32[128,10,256]{2,0,1:T(8,128)} fusion(bf16[128,10,3584]{2,0,1:T(8,128)(2,1)} %bitcast.237, bf16[1,3584,256]{2,1,0:T(8,128)(2,1)} %param.19), kind=kOutput, calls=%fused_computation.40 | convolution fusion | flops 2348810240 | bytes 12320768 | tf_op jit(solution)/shard_map/smd,df->smf/dot_general | solution.py:110
  453.6 18.5 %convolution_convert_fusion = bf16[128,10,3584]{2,0,1:T(8,128)(2,1)} fusion(bf16[1,256,3584]{2,1,0:T(8,128)(2,1)S(1)} %copy-done, bf16[128,10,3584]{2,0,1:T(8,128)(2,1)} %bitcast.238, bf16[1,3584,256]{2,1,0:T(8,128)(2,1)} %param.20, f32[128,10,256]{2,0,1:T(8,128)} %fusion.28), kind=kOutput, calls=%fused_computation.14 | convolution fusion | flops 4704174080 | bytes 23330816 | tf_op jit(solution)/shard_map/smf,fd->smd/dot_general | solution.py:114
  472.1 78.5 %reduce-scatter.5.cloned.1.call-done = bf16[32,10,3584]{2,0,1:T(8,128)(2,1)} async-done(((bf16[128,10,3584]{2,0,1:T(8,128)(2,1)}), bf16[32,10,3584]{2,0,1:T(8,128)(2,1)}) %reduce-scatter.5.cloned.1.call-update) | async-done | bytes 2293776 | tf_op jit(solution)/shard_map/reduce_scatter | solution.py:113
  550.6 4.9 copy.68
  555.5 7.4 %all-to-all-start.2 = ((bf16[32,10,3584]{2,1,0:T(8,128)(2,1)}), bf16[32,10,3584]{2,1,0:T(8,128)(2,1)}, u32[]{:S(2)}, u32[]{:S(2)}) async-start(bf16[32,10,3584]{2,1,0:T(8,128)(2,1)} %copy.68), calls=%async_computation.4 | async-start | bytes 7340032 | tf_op jit(solution)/shard_map/all_to_all | solution.py:121
  563.4 49.3 %all-to-all-done.2 = bf16[32,10,3584]{2,1,0:T(8,128)(2,1)} async-done(((bf16[32,10,3584]{2,1,0:T(8,128)(2,1)}), bf16[32,10,3584]{2,1,0:T(8,128)(2,1)}, u32[]{:S(2)}, u32[]{:S(2)}) %all-to-all-start.2) | async-done | bytes 2293792 | tf_op jit(solution)/shard_map/all_to_all | solution.py:121
  612.6 4.5 reshape.103
  617.1 3.6 fusion.12
  (54 shorter events, 24.1 us)
Async XLA Ops:
  6.5 447.1 %copy-start = (bf16[1,256,3584]{2,1,0:T(8,128)(2,1)S(1)}, bf16[1,256,3584]{2,1,0:T(8,128)(2,1)}, u32[]{:S(2)}) copy-start(bf16[1,256,3584]{2,1,0:T(8,128)(2,1)} %param.21) | copy-start | bytes 5505028
  6.5 276.5 %reduce-scatter.3.cloned.1.call-start = ((), (), s32[]{:S(2)}) async-start(), calls=%async_computation.5 | async-start | bytes 7569408 | tf_op jit(solution)/shard_map/reduce_scatter | solution.py:69
  9.2 37.1 %copy-start.1 = (bf16[1024,256]{1,0:T(8,128)(2,1)S(1)}, bf16[1024,256]{1,0:T(8,128)(2,1)}, u32[]{:S(2)}) copy-start(bf16[1024,256]{1,0:T(8,128)(2,1)} %param.11) | copy-start | bytes 1572868
  9.3 3.8 collective-permute-start
  13.1 23.9 %collective-permute-start.1 = (bf16[2,1024,256]{1,2,0:T(8,128)(2,1)}, bf16[2,1024,256]{1,2,0:T(8,128)(2,1)}, u32[]{:S(2)}, u32[]{:S(2)}) collective-permute-start(bf16[2,1024,256]{1,2,0:T(8,128)(2,1)} %collective-permute-done), channel_id=1, source_target_pairs={{0,32},{32,64},{64,96},{1,33},{33,65},{65,97},{2,34},{34,66},{66,9... | collective-permute-start | bytes 3145736 | tf_op jit(solution)/shard_map/ppermute | solution.py:15
  37.1 13.4 %collective-permute-start.2 = (bf16[2,1024,256]{1,2,0:T(8,128)(2,1)}, bf16[2,1024,256]{1,2,0:T(8,128)(2,1)S(1)}, u32[]{:S(2)}, u32[]{:S(2)}) collective-permute-start(bf16[2,1024,256]{1,2,0:T(8,128)(2,1)} %collective-permute-done.1), channel_id=1, source_target_pairs={{0,32},{32,64},{64,96},{1,33},{33,65},{65,97},{2,34},{34,66},{66,9... | collective-permute-start | bytes 3145736 | tf_op jit(solution)/shard_map/ppermute | solution.py:15
  73.0 2.4 copy-start.4
  75.4 5.2 copy-start.6
  75.4 207.6 %copy-start.2 = (bf16[32,3584]{1,0:T(8,128)(2,1)S(1)}, bf16[32,3584]{1,0:T(8,128)(2,1)}, u32[]{:S(2)}) copy-start(bf16[32,3584]{1,0:T(8,128)(2,1)} %param.15) | copy-start | bytes 688132
  75.5 208.8 %copy-start.5 = (f32[3584]{0:T(1024)S(1)}, f32[3584]{0:T(1024)}, u32[]{:S(2)}) copy-start(f32[3584]{0:T(1024)} %param.16) | copy-start | bytes 43012
  80.6 470.0 %reduce-scatter.5.cloned.1.call-start = ((), (), s32[]{:S(2)}) async-start(), calls=%async_computation.6 | async-start | bytes 11468800 | tf_op jit(solution)/shard_map/reduce_scatter | solution.py:113
  472.1 90.7 %copy-start.7 = (f32[32,8]{0,1:T(8,128)S(1)}, f32[32,8]{0,1:T(8,128)}, u32[]{:S(2)}) copy-start(f32[32,8]{0,1:T(8,128)} %param.18) | copy-start | bytes 3076
  472.1 145.0 %copy-start.3 = (bf16[32,3584]{1,0:T(8,128)(2,1)S(1)}, bf16[32,3584]{1,0:T(8,128)(2,1)}, u32[]{:S(2)}) copy-start(bf16[32,3584]{1,0:T(8,128)(2,1)} %reduce-scatter.3.cloned.1.call-done) | copy-start | bytes 688132
  555.5 57.2 %all-to-all-start.2 = ((bf16[32,10,3584]{2,1,0:T(8,128)(2,1)}), bf16[32,10,3584]{2,1,0:T(8,128)(2,1)}, u32[]{:S(2)}, u32[]{:S(2)}) async-start(bf16[32,10,3584]{2,1,0:T(8,128)(2,1)} %copy.68), calls=%async_computation.4 | async-start | bytes 7340032 | tf_op jit(solution)/shard_map/all_to_all | solution.py:121
Sparse Core Ops, SparseCore 0:
  80.7 202.3 reduce-scatter.2
  472.2 78.3 reduce-scatter.4
